TPU v7x, 256 devices: a whole 4x4x8 slice. The times are simulated.
256 devices in a mesh: ctx: 8 (over y, x_hi), ch: 32 (over z, x_lo, core).
Axes of the slice: x: 4 (x_hi: 2, x_lo: 2; x = x_hi * 2 + x_lo), y: 4, z: 8, core: 2. Of those that a mesh axis runs over, the one named last changes fastest.
Arguments:
- gate_act: bfloat16 [4096, 8192], P('ctx', 'ch'), may hold values from -6 to 6
- key_act: bfloat16 [4096, 8192], P('ctx', 'ch'), may hold values from -6 to 6
- value_act: bfloat16 [4096, 8192], P('ctx', 'ch'), may hold values from -6 to 6
- filter_taps: float32 [6144, 8192], P('ctx', 'ch'), may hold values from -2 to 2
- skip_gain: float32 [8192], P('ch'), may hold values from 0.5 to 1.5
- w_out: bfloat16 [8192, 8192], P(None, 'ch'), may hold values from -0.0625 to 0.0625
- span_order: int32 [16], replicated, may hold values from 0 to 15, each once
- decode_order: int32 [8], replicated, may hold values from 0 to 7, each once
Outputs:
- projected: bfloat16 [4096, 8192], P('ctx', 'ch')
- tail: float32 [2048, 8192], P('ctx', 'ch')
Inputs may be any that keep to these rules, and one draw needn't show every extreme that they name: `span_order`: each span number once. `decode_order`: each future block number once.
All inputs are finite; a program needn't handle non-finite values.
Results may differ from a plain program's by a relative error of at most 0.017.
Values may be sent and summed in bfloat16 or wider, within the bound.
No kernel may reach another device: no remote copies, remote signals or barrier semaphores. Data moves between devices by JAX's collectives and lax.ppermute only.
A program may use at most 128 MiB of HBM per device.

v0:
```python
import math
import jax
import jax.numpy as jnp
from jax import lax
from jax.sharding import PartitionSpec as P

SPAN = 256
HIGH = lax.Precision.HIGH


def forward_table(length):
    half = length // 2
    rows_idx = lax.broadcasted_iota(jnp.int32, (length, length), 0)
    cols_idx = lax.broadcasted_iota(jnp.int32, (length, length), 1)
    frequency = rows_idx % half
    phase = (frequency * cols_idx % length).astype(jnp.float32) * (2.0 * math.pi / length)
    parity = (1 - 2 * (cols_idx % 2)).astype(jnp.float32)
    table = jnp.where(rows_idx < half, jnp.cos(phase), -jnp.sin(phase))
    return jnp.where(rows_idx == half, parity, table)


def inverse_table(length):
    half = length // 2
    rows_idx = lax.broadcasted_iota(jnp.int32, (half, length), 0)
    cols_idx = lax.broadcasted_iota(jnp.int32, (half, length), 1)
    frequency = cols_idx % half
    phase = (frequency * rows_idx % length).astype(jnp.float32) * (2.0 * math.pi / length)
    weight = jnp.where(frequency == 0, 1.0 / length, 2.0 / length)
    table = jnp.where(cols_idx < half, weight * jnp.cos(phase), -weight * jnp.sin(phase))
    parity = (1 - 2 * (rows_idx % 2)).astype(jnp.float32) / length
    return jnp.where(cols_idx == half, parity, table)


def spectral_product(left, right):
    half = left.shape[-2] // 2
    left_re, left_im = (left[..., :half, :], left[..., half:, :])
    right_re, right_im = (right[..., :half, :], right[..., half:, :])
    first = lax.broadcasted_iota(jnp.int32, left_re.shape, left_re.ndim - 2) == 0
    real_part = jnp.where(first, left_re * right_re, left_re * right_re - left_im * right_im)
    imag_part = jnp.where(first, left_im * right_im, left_re * right_im + left_im * right_re)
    return jnp.concatenate([real_part, imag_part], axis=-2)


def per_device(
    gate_act, key_act, value_act, filter_taps, skip_gain, w_out, span_order, decode_order
):
    width = gate_act.shape[1]
    length = 2 * SPAN
    cycle_size = lax.axis_size("ctx")
    position = lax.axis_index("ctx")
    count_spans = 2 * cycle_size
    count_lags = 3 * cycle_size
    forward = forward_table(length).astype(jnp.bfloat16)
    inverse = inverse_table(length)
    signal = (key_act.astype(jnp.float32) * value_act.astype(jnp.float32)).astype(jnp.bfloat16)
    all_taps = lax.all_gather(filter_taps.astype(jnp.bfloat16), "ctx", axis=0, tiled=True)
    blocks = all_taps.reshape(count_lags, SPAN, width)
    earlier = jnp.concatenate([jnp.zeros((1, SPAN, width), jnp.bfloat16), blocks[:-1]], axis=0)
    seg_spec = jnp.einsum(
        "kn,anc->akc", forward[:, :SPAN], blocks, preferred_element_type=jnp.float32
    ) + jnp.einsum(
        "kn,anc->akc", forward[:, SPAN + 1 :], earlier[:, 1:, :], preferred_element_type=jnp.float32
    )
    piece = lax.all_gather(signal, "ctx", axis=0, tiled=True)
    span_spec = jnp.einsum(
        "kn,anc->akc",
        forward[:, :SPAN],
        piece.reshape(count_spans, SPAN, width),
        preferred_element_type=jnp.float32,
    )
    my_spans = lax.dynamic_slice_in_dim(span_order, 2 * position, 2)
    my_future = count_spans + lax.dynamic_index_in_dim(decode_order, position, keepdims=False)
    targets = jnp.concatenate([my_spans, my_future[None]])
    lags = targets[:, None] - span_order[None, :]
    picked = jnp.take(seg_spec, jnp.maximum(lags, 0), axis=0)
    terms = spectral_product(picked, span_spec[None])
    totals = jnp.sum(jnp.where((lags >= 0)[:, :, None, None], terms, 0.0), axis=1)
    blocks_out = jnp.einsum(
        "nk,akc->anc", inverse, totals, precision=HIGH, preferred_element_type=jnp.float32
    )
    conv = blocks_out[:2].reshape(2 * SPAN, width)
    tail = blocks_out[2]
    mixed = (
        gate_act.astype(jnp.float32) * (conv + skip_gain[None, :] * signal.astype(jnp.float32))
    ).astype(jnp.bfloat16)
    summed = jnp.dot(
        lax.all_gather(mixed, "ch", axis=1, tiled=True), w_out, preferred_element_type=jnp.float32
    )
    projected = summed.astype(jnp.bfloat16)
    return (projected, tail)


def solution(mesh):
    in_specs = (
        P("ctx", "ch"),
        P("ctx", "ch"),
        P("ctx", "ch"),
        P("ctx", "ch"),
        P("ch"),
        P(None, "ch"),
        P(),
        P(),
    )
    out_specs = (P("ctx", "ch"), P("ctx", "ch"))
    return jax.shard_map(
        per_device, mesh=mesh, in_specs=in_specs, out_specs=out_specs, check_vma=False
    )
```

profile of v0, /device:TPU:1, one launch (start us, length us, event | category | flops | bytes accessed | tf_op | source)
XLA Modules:
  0.0 318.4 jit_solution(5243990914818297299)
XLA Ops:
  7.2 0.0 all-gather.6.cloned.1.call-start
  7.2 1.8 multiply_convert_fusion
  9.0 0.0 all-gather.6.cloned.1.call-update
  9.0 0.0 all-gather.4.cloned.1.call-start
  9.1 1.9 convert_element_type.55
  11.0 0.0 all-gather.4.cloned.1.call-update
  11.0 0.0 all-gather.8.cloned.1.call-start
  11.1 0.7 dynamic_slice.7
  11.8 1.2 dynamic_slice.8
  13.7 0.1 pad_add_fusion
  13.8 0.7 subtract_maximum_fusion.1
  14.5 0.1 reshape.110
  14.6 0.5 iota_compare_fusion.2
  15.1 0.6 compare_and_fusion
  15.7 0.6 iota_and_fusion.2
  16.4 0.7 subtract_compare_fusion
  17.1 5.0 %select_convert_fusion = bf16[512,512]{1,0:T(8,128)(2,1)S(1)} fusion(s32[512]{0:T(512)S(1)} %get-tuple-element.8, s32[512]{0:T(512)S(1)} %get-tuple-element.9, s32[512]{0:T(512)S(1)} %get-tuple-element.12, s32[512]{0:T(512)S(1)} %get-tuple-element.13, pred[512]{0:T(512)(128)(4,1)S(1)} %get-tuple-element.15, pred[512]{0:T(512)(128)(4,1)S(1)} %get-tuple-element.10, ...), kind=kLoop, calls=%fused_computation.21 | loop fusion | flops 6029312 | bytes 534528 | tf_op jit(solution)/shard_map/convert_element_type | solution.py:53
  22.1 50.8 %all-gather.6.cloned.1.call-done = bf16[4096,256]{1,0:T(8,128)(2,1)} async-done(((bf16[512,256]{1,0:T(8,128)(2,1)}), bf16[4096,256]{1,0:T(8,128)(2,1)}) %all-gather.6.cloned.1.call-update) | async-done | bytes 2097168 | tf_op jit(solution)/shard_map/all_gather | solution.py:64
  72.9 2.9 convolution_bitcast_fusion
  75.8 4.2 %slice_bitcast_fusion.1 = (f32[16,256,256]{1,2,0:T(8,128)}, f32[16,256,256]{1,2,0:T(8,128)}) fusion(f32[1,16,512,256]{2,3,1,0:T(8,128)S(1)} %convolution_bitcast_fusion), kind=kLoop, calls=%fused_computation.9 | loop fusion | bytes 16777216 | tf_op jit(solution)/shard_map/mul | solution.py:39
  80.0 0.0 copy-done.3
  80.0 5.4 %copy.16 = f32[16,256,256]{2,1,0:T(8,128)} copy(f32[16,256,256]{1,2,0:T(8,128)} %get-tuple-element.4) | data formatting | bytes 8388608 | tf_op jit(solution)/shard_map/mul | solution.py:39
  85.5 5.5 %copy.17 = f32[16,256,256]{2,1,0:T(8,128)} copy(f32[16,256,256]{1,2,0:T(8,128)} %get-tuple-element.5) | data formatting | bytes 8388608 | tf_op jit(solution)/shard_map/mul | solution.py:39
  91.0 49.8 %all-gather.4.cloned.1.call-done = bf16[6144,256]{1,0:T(8,128)(2,1)} async-done(((bf16[768,256]{1,0:T(8,128)(2,1)}), bf16[6144,256]{1,0:T(8,128)(2,1)}) %all-gather.4.cloned.1.call-update) | async-done | bytes 3145744 | tf_op jit(solution)/shard_map/all_gather | solution.py:56
  140.7 8.4 %fusion.44 = f32[512,24,256]{2,0,1:T(8,128)} fusion(bf16[24,256,256]{2,1,0:T(8,128)(2,1)} %bitcast.44, bf16[512,512]{1,0:T(8,128)(2,1)S(1)} %select_convert_fusion), kind=kOutput, calls=%fused_computation.69 | convolution fusion | flops 1610612736 | bytes 15990784 | tf_op jit(solution)/shard_map/kn,anc->akc/dot_general | solution.py:59
  149.2 0.0 copy-done
  149.2 1.8 slice.50
  151.0 3.4 %copy.13 = bf16[23,256,256]{1,2,0:T(8,128)(2,1)S(1)} copy(bf16[23,256,256]{2,1,0:T(8,128)(2,1)} %bitcast.45) | data formatting | bytes 6029312 | tf_op jit(solution)/shard_map/slice | solution.py:58
  154.4 11.0 %bitcast_add_fusion = f32[24,512,256]{2,1,0:T(8,128)} fusion(f32[512,24,256]{2,0,1:T(8,128)} %fusion.44, bf16[23,256,256]{1,2,0:T(8,128)(2,1)S(1)} %copy.13, bf16[512,512]{1,0:T(8,128)(2,1)S(1)} %select_convert_fusion), kind=kOutput, calls=%fused_computation.4 | convolution fusion | flops 1607467008 | bytes 28442624 | tf_op jit(solution)/shard_map/kn,anc->akc/dot_general | solution.py:61
  165.4 15.2 %gather_fusion = f32[48,512,256]{2,1,0:T(8,128)} fusion(f32[24,512,256]{2,1,0:T(8,128)} %bitcast_add_fusion, s32[1024]{0:T(1024)S(1)} %pad_clamp_fusion), kind=kCustom, calls=%fused_computation | custom fusion | bytes 50331840 | tf_op jit(solution)/shard_map/jit(_take)/gather | solution.py:75
  180.7 9.8 %broadcast_select_fusion = f32[3,16,512,256]{3,2,1,0:T(8,128)S(1)} fusion(f32[3,16,512,256]{3,2,1,0:T(8,128)} %bitcast.43, pred[3,16]{1,0:T(4,128)(4,1)S(1)} %get-tuple-element.7), kind=kLoop, calls=%fused_computation.6 | loop fusion | flops 6291456 | bytes 50331696 | tf_op jit(solution)/shard_map/jit(_take)/select_n | solution.py:75
  190.5 0.0 copy-done.8
  190.5 12.4 %subtract_select_fusion = (f32[3,16,256,256]{3,2,1,0:T(8,128)}, f32[3,16,256,256]{3,2,1,0:T(8,128)}) fusion(f32[3,16,512,256]{3,2,1,0:T(8,128)S(1)} %broadcast_select_fusion, f32[16,256,256]{2,1,0:T(8,128)} %copy.17, f32[16,256,256]{2,1,0:T(8,128)} %copy.16, pred[256]{0:T(512)(128)(4,1)S(1)} %copy-done.8), kind=kLoop, calls=%fused_computation.3 | loop fusion | flops 25165824 | bytes 58720512 | tf_op jit(solution)/shard_map/jit(_where)/select_n | solution.py:39
  202.8 0.0 copy-start.10
  202.9 0.0 copy-start.12
  202.9 0.0 copy-start.14
  202.9 0.0 copy-start.15
  202.9 0.0 copy-start.1
  202.9 0.0 copy-start.2
  202.9 0.0 copy-start.7
  202.9 9.9 %fusion = f32[3,512,256]{2,1,0:T(8,128)S(1)} fusion(f32[3,16,256,256]{3,2,1,0:T(8,128)} %get-tuple-element.3, f32[3,16,256,256]{3,2,1,0:T(8,128)} %get-tuple-element.2, pred[3,16]{1,0:T(4,128)(4,1)S(1)} %get-tuple-element.6), kind=kLoop, calls=%fused_computation.2 | loop fusion | flops 18481152 | bytes 26738736 | tf_op jit(solution)/shard_map/reduce_sum | solution.py:77
  212.9 3.0 convolution_bitcast_fusion.1
  215.9 0.0 copy-done.1
  215.9 0.8 fusion.16
  216.7 0.0 all-gather.8.cloned.1.call-update
  216.8 0.7 slice_bitcast_fusion.2
  217.5 86.8 %all-gather.8.cloned.1.call-done = bf16[512,8192]{1,0:T(8,128)(2,1)} async-done(((bf16[512,256]{1,0:T(8,128)(2,1)}), bf16[512,8192]{1,0:T(8,128)(2,1)}) %all-gather.8.cloned.1.call-update) | async-done | bytes 8388624 | tf_op jit(solution)/shard_map/all_gather | solution.py:87
  304.3 7.6 %convolution_convert_fusion = bf16[512,256]{1,0:T(8,128)(2,1)} fusion(bf16[512,8192]{1,0:T(8,128)(2,1)} %all-gather.8.cloned.1.call-done, bf16[8192,256]{1,0:T(8,128)(2,1)} %param.13), kind=kOutput, calls=%fused_computation.17 | convolution fusion | flops 2147614720 | bytes 12845056 | tf_op jit(solution)/shard_map/dot_general | solution.py:86
  (27 shorter events, 0.1 us)
Async XLA Ops:
  7.2 65.7 %all-gather.6.cloned.1.call-start = ((), (), s32[]{:S(2)}) async-start(), calls=%async_computation.1 | async-start | bytes 2359296 | tf_op jit(solution)/shard_map/all_gather | solution.py:64
  9.0 131.7 %all-gather.4.cloned.1.call-start = ((), (), s32[]{:S(2)}) async-start(), calls=%async_computation | async-start | bytes 3538944 | tf_op jit(solution)/shard_map/all_gather | solution.py:56
  11.0 293.3 %all-gather.8.cloned.1.call-start = ((), (), s32[]{:S(2)}) async-start(), calls=%async_computation.2 | async-start | bytes 8650752 | tf_op jit(solution)/shard_map/all_gather | solution.py:87
  15.7 64.3 %copy-start.9 = (pred[512]{0:T(512)(128)(4,1)}, pred[512]{0:T(512)(128)(4,1)S(1)}, u32[]{:S(2)}) copy-start(pred[512]{0:T(512)(128)(4,1)S(1)} %get-tuple-element.10) | copy-start | bytes 1540
  15.7 64.3 %copy-start.11 = (pred[512]{0:T(512)(128)(4,1)}, pred[512]{0:T(512)(128)(4,1)S(1)}, u32[]{:S(2)}) copy-start(pred[512]{0:T(512)(128)(4,1)S(1)} %get-tuple-element.11) | copy-start | bytes 1540
  15.7 64.3 %copy-start.13 = (pred[512]{0:T(512)(128)(4,1)}, pred[512]{0:T(512)(128)(4,1)S(1)}, u32[]{:S(2)}) copy-start(pred[512]{0:T(512)(128)(4,1)S(1)} %get-tuple-element.15) | copy-start | bytes 1540
  16.3 63.7 %copy-start.3 = (s32[512]{0:T(512)}, s32[512]{0:T(512)S(1)}, u32[]{:S(2)}) copy-start(s32[512]{0:T(512)S(1)} %get-tuple-element.9) | copy-start | bytes 6148
  140.7 8.4 %copy-start = (bf16[6144,256]{1,0:T(8,128)(2,1)S(1)}, bf16[6144,256]{1,0:T(8,128)(2,1)}, u32[]{:S(2)}) copy-start(bf16[6144,256]{1,0:T(8,128)(2,1)} %all-gather.4.cloned.1.call-done) | copy-start | bytes 9437188
  180.7 9.8 %copy-start.8 = (pred[256]{0:T(512)(128)(4,1)S(1)}, pred[256]{0:T(512)(128)(4,1)}, u32[]{:S(2)}) copy-start(pred[256]{0:T(512)(128)(4,1)} %iota_compare_fusion.2) | copy-start | bytes 772
  202.8 10.0 %copy-start.4 = (s32[512]{0:T(512)S(1)}, s32[512]{0:T(512)}, u32[]{:S(2)}) copy-start(s32[512]{0:T(512)} %copy-done.3) | copy-start | bytes 6148
  202.8 10.0 %copy-start.5 = (s32[256]{0:T(256)S(1)}, s32[256]{0:T(256)}, u32[]{:S(2)}) copy-start(s32[256]{0:T(256)} %get-tuple-element.16) | copy-start | bytes 3076
  202.8 10.0 %copy-start.6 = (s32[256]{0:T(256)S(1)}, s32[256]{0:T(256)}, u32[]{:S(2)}) copy-start(s32[256]{0:T(256)} %get-tuple-element.17) | copy-start | bytes 3076
  202.8 10.0 %copy-start.10 = (pred[512]{0:T(512)(128)(4,1)S(1)}, pred[512]{0:T(512)(128)(4,1)}, u32[]{:S(2)}) copy-start(pred[512]{0:T(512)(128)(4,1)} %copy-done.9) | copy-start | bytes 1540
  202.9 10.0 %copy-start.12 = (pred[512]{0:T(512)(128)(4,1)S(1)}, pred[512]{0:T(512)(128)(4,1)}, u32[]{:S(2)}) copy-start(pred[512]{0:T(512)(128)(4,1)} %copy-done.11) | copy-start | bytes 1540
  202.9 10.0 %copy-start.14 = (pred[512]{0:T(512)(128)(4,1)S(1)}, pred[512]{0:T(512)(128)(4,1)}, u32[]{:S(2)}) copy-start(pred[512]{0:T(512)(128)(4,1)} %copy-done.13) | copy-start | bytes 1540
  202.9 10.0 %copy-start.15 = (pred[256]{0:T(512)(128)(4,1)S(1)}, pred[256]{0:T(512)(128)(4,1)}, u32[]{:S(2)}) copy-start(pred[256]{0:T(512)(128)(4,1)} %compare_and_fusion) | copy-start | bytes 772
  202.9 13.0 %copy-start.1 = (bf16[512,256]{1,0:T(8,128)(2,1)S(1)}, bf16[512,256]{1,0:T(8,128)(2,1)}, u32[]{:S(2)}) copy-start(bf16[512,256]{1,0:T(8,128)(2,1)} %multiply_convert_fusion) | copy-start | bytes 786436
  202.9 13.0 %copy-start.2 = (bf16[512,256]{1,0:T(8,128)(2,1)S(1)}, bf16[512,256]{1,0:T(8,128)(2,1)}, u32[]{:S(2)}) copy-start(bf16[512,256]{1,0:T(8,128)(2,1)} %param.8) | copy-start | bytes 786436
  202.9 13.0 %copy-start.7 = (f32[256]{0:T(256)S(1)}, f32[256]{0:T(256)}, u32[]{:S(2)}) copy-start(f32[256]{0:T(256)} %param.12) | copy-start | bytes 3076
Sparse Core Ops, SparseCore 0:
  11.2 61.6 all-gather.5
  75.5 65.1 all-gather.3
  216.9 87.3 all-gather.7
where the time goes:
time: 319 us; the launch traced here: 318 us
  waiting for transfers between devices  187 us (59%)
  other arithmetic  44.8 us (14%)
  local copies, waits for them, and re-layouts  38.4 us (12%)
  matrix products  32.9 us (10%)
  between operations  14.7 us (5%)
    all_gather x1, waiting for transfers between devices, per_device(): lax.all_gather(mixed, 'ch', axis=1, tiled=True)  86.8 us
    all_gather x1, waiting for transfers between devices, per_device(): piece = lax.all_gather(signal, 'ctx', axis=0, tiled=True)  50.8 us
    all_gather x1, waiting for transfers between devices, per_device(): lax.all_gather(filter_taps.astype(jnp.bfloat16), 'ctx', axis=0, tiled=True)  49.8 us
    gather x1, local copies, waits for them, and re-layouts, per_device(): picked = jnp.take(seg_spec, jnp.maximum(lags, 0), axis=0)  15.2 us
    select_n x1, other arithmetic, spectral_product(): jnp.where(first, left_re * right_re, left_re * right_re - left_im * right...  12.4 us
    dot_general x1, matrix products, per_device(): jnp.einsum('kn,anc->akc', forward[:, SPAN + 1:], earlier[:, 1:, :], prefe...  11 us
    reduce_sum x1, other arithmetic, per_device(): jnp.sum(jnp.where((lags >= 0)[:, :, None, None], terms, 0.0), axis=1)  9.87 us
    select_n x1, other arithmetic, per_device(): picked = jnp.take(seg_spec, jnp.maximum(lags, 0), axis=0)  9.8 us
  transfers between devices with their start and end apart: 3, of which 3 were waited for; matrix products, arithmetic and copies ran while one was open for 10% of the time, Pallas kernels for 0%

commit v1 on v0

--- a/solution.py
+++ b/solution.py
@@ -53,7 +53,12 @@
     forward = forward_table(length).astype(jnp.bfloat16)
     inverse = inverse_table(length)
     signal = (key_act.astype(jnp.float32) * value_act.astype(jnp.float32)).astype(jnp.bfloat16)
-    all_taps = lax.all_gather(filter_taps.astype(jnp.bfloat16), "ctx", axis=0, tiled=True)
+    all_taps = jnp.concatenate(
+        lax.all_to_all(
+            jnp.stack([filter_taps.astype(jnp.bfloat16)] * lax.axis_size("ctx")), "ctx", 0, 0
+        ),
+        axis=0,
+    )
     blocks = all_taps.reshape(count_lags, SPAN, width)
     earlier = jnp.concatenate([jnp.zeros((1, SPAN, width), jnp.bfloat16), blocks[:-1]], axis=0)
     seg_spec = jnp.einsum(

time: 319 us -> 243 us (0.76)
  waiting for transfers between devices: 187 us -> 122 us
  matrix products: 32.9 us -> 22.9 us
  starting transfers between devices: 0.12 us -> 7.55 us
  local copies, waits for them, and re-layouts: 38.4 us -> 33.7 us
    all_gather x1, waiting for transfers between devices: 50.8 us -> 0.01 us  [per_device(): piece = lax.all_gather(signal, 'ctx', axis=0, tiled=True)]
    all_gather x1 -> x0, waiting for transfers between devices: 49.8 us -> none  [per_device(): lax.all_gather(filter_taps.astype(jnp.bfloat16), 'ctx', axis=0, tiled=True)]
    all_to_all x0 -> x1, waiting for transfers between devices: none -> 32.4 us  [per_device(): lax.all_to_all(jnp.stack([filter_taps.astype(jnp.bfloat16)] * lax.axis_si...]
    select_n x1, other arithmetic: 9.8 us -> 17.5 us  [per_device(): picked = jnp.take(seg_spec, jnp.maximum(lags, 0), axis=0)]
    all_to_all x0 -> x1, starting transfers between devices: none -> 7.47 us  [per_device(): lax.all_to_all(jnp.stack([filter_taps.astype(jnp.bfloat16)] * lax.axis_si...]
    reduce_sum x1, other arithmetic: 9.87 us -> 2.62 us  [per_device(): jnp.sum(jnp.where((lags >= 0)[:, :, None, None], terms, 0.0), axis=1)]
    dot_general x1, matrix products: 8.44 us -> 2.82 us  [per_device(): jnp.einsum('kn,anc->akc', forward[:, :SPAN], blocks, preferred_element_ty...]
    slice x2 -> x1, local copies, waits for them, and re-layouts: 5.23 us -> 0.2 us  [per_device(): blocks[:-1]]
  transfers between devices with their start and end apart: 3 -> 3, of which waited for: 3 -> 2; matrix products, arithmetic and copies ran while one was open for 10% -> 21% of each run, Pallas kernels for 0% -> 0%
where the time goes in v1:
time: 243 us; the launch traced here: 242 us
  waiting for transfers between devices  122 us (50%)
  other arithmetic  41.7 us (17%)
  local copies, waits for them, and re-layouts  33.7 us (14%)
  matrix products  22.9 us (9%)
  between operations  14.9 us (6%)
  starting transfers between devices  7.55 us (3%)
    all_gather x1, waiting for transfers between devices, per_device(): lax.all_gather(mixed, 'ch', axis=1, tiled=True)  89.3 us
    all_to_all x1, waiting for transfers between devices, per_device(): lax.all_to_all(jnp.stack([filter_taps.astype(jnp.bfloat16)] * lax.axis_si...  32.4 us
    select_n x1, other arithmetic, per_device(): picked = jnp.take(seg_spec, jnp.maximum(lags, 0), axis=0)  17.5 us
    gather x1, local copies, waits for them, and re-layouts, per_device(): picked = jnp.take(seg_spec, jnp.maximum(lags, 0), axis=0)  15.2 us
    select_n x1, other arithmetic, spectral_product(): jnp.where(first, left_re * right_re, left_re * right_re - left_im * right...  11.9 us
    mul x2, local copies, waits for them, and re-layouts, spectral_product(): left_re * right_re  9.5 us
    dot_general x1, matrix products, per_device(): jnp.dot(lax.all_gather(mixed, 'ch', axis=1, tiled=True), w_out, preferred...  7.6 us
    all_to_all x1, starting transfers between devices, per_device(): lax.all_to_all(jnp.stack([filter_taps.astype(jnp.bfloat16)] * lax.axis_si...  7.47 us
  transfers between devices with their start and end apart: 3, of which 2 were waited for; matrix products, arithmetic and copies ran while one was open for 21% of the time, Pallas kernels for 0%

profile of v1, /device:TPU:1, one launch (start us, length us, event | category | flops | bytes accessed | tf_op | source)
XLA Modules:
  0.0 242.5 jit_solution(4266550316189653021)
XLA Ops:
  7.2 0.0 copy-start.3
  7.2 0.0 copy-start.5
  7.2 0.0 copy-start.7
  7.2 1.2 convert_element_type.55
  8.4 1.9 stack.2
  10.3 7.5 %all-to-all-start = ((bf16[8,768,256]{2,1,0:T(8,128)(2,1)}), bf16[8,768,256]{2,1,0:T(8,128)(2,1)S(1)}, u32[]{:S(2)}, u32[]{:S(2)}) async-start(bf16[8,768,256]{2,1,0:T(8,128)(2,1)} %stack.2), calls=%async_computation | async-start | bytes 6291456 | tf_op jit(solution)/shard_map/all_to_all | solution.py:57
  17.7 0.0 all-gather.3.cloned.1.call-start
  17.8 0.0 copy-done.3
  17.8 1.7 multiply_convert_fusion
  19.5 0.0 all-gather.3.cloned.1.call-update
  19.5 0.0 all-gather.5.cloned.1.call-start
  19.6 0.0 copy-done.5
  19.6 0.1 dynamic_slice.7
  19.7 0.0 copy-done.7
  19.7 0.6 dynamic_slice.8
  20.9 0.1 pad_add_fusion
  21.0 0.1 subtract_maximum_fusion.1
  21.1 0.1 reshape.107
  21.2 5.7 %select_convert_fusion = bf16[512,512]{1,0:T(8,128)(2,1)} fusion(s32[512]{0:T(512)S(1)} %get-tuple-element.8, s32[512]{0:T(512)S(1)} %get-tuple-element.9, s32[512]{0:T(512)S(1)} %get-tuple-element.12, s32[512]{0:T(512)S(1)} %get-tuple-element.13, pred[512]{0:T(512)(128)(4,1)S(1)} %get-tuple-element.15, pred[512]{0:T(512)(128)(4,1)S(1)} %get-tuple-element.10, ...), kind=kLoop, calls=%fused_computation.21 | loop fusion | flops 6029312 | bytes 534528 | tf_op jit(solution)/shard_map/convert_element_type | solution.py:53
  26.9 0.1 subtract_compare_fusion
  27.0 32.4 %all-to-all-done = bf16[8,768,256]{2,1,0:T(8,128)(2,1)S(1)} async-done(((bf16[8,768,256]{2,1,0:T(8,128)(2,1)}), bf16[8,768,256]{2,1,0:T(8,128)(2,1)S(1)}, u32[]{:S(2)}, u32[]{:S(2)}) %all-to-all-start) | async-done | bytes 3145760 | tf_op jit(solution)/shard_map/all_to_all | solution.py:57
  59.4 0.2 slice.46
  59.6 0.0 copy-start.1
  59.6 2.8 %fusion.44 = f32[512,24,256]{2,0,1:T(8,128)S(1)} fusion(bf16[24,256,256]{2,1,0:T(8,128)(2,1)S(1)} %bitcast.44, bf16[512,512]{1,0:T(8,128)(2,1)} %select_convert_fusion), kind=kOutput, calls=%fused_computation.69 | convolution fusion | flops 1610612736 | bytes 15990784 | tf_op jit(solution)/shard_map/kn,anc->akc/dot_general | solution.py:64
  62.4 0.0 copy-done.1
  62.4 6.6 %bitcast_add_fusion = f32[24,512,256]{2,1,0:T(8,128)} fusion(f32[512,24,256]{2,0,1:T(8,128)S(1)} %fusion.44, bf16[23,256,256]{2,1,0:T(8,128)(2,1)S(1)} %slice.46, bf16[512,512]{1,0:T(8,128)(2,1)S(1)} %copy-done.1), kind=kOutput, calls=%fused_computation.4 | convolution fusion | flops 1607467008 | bytes 28442624 | tf_op jit(solution)/shard_map/kn,anc->akc/dot_general | solution.py:66
  69.0 15.2 %gather_fusion = f32[48,512,256]{2,1,0:T(8,128)} fusion(f32[24,512,256]{2,1,0:T(8,128)} %bitcast_add_fusion, s32[1024]{0:T(1024)S(1)} %pad_clamp_fusion), kind=kCustom, calls=%fused_computation | custom fusion | bytes 50331840 | tf_op jit(solution)/shard_map/jit(_take)/gather | solution.py:80
  84.2 0.0 copy-start.2
  84.2 17.5 %broadcast_select_fusion = f32[3,16,512,256]{3,2,1,0:T(8,128)} fusion(f32[3,16,512,256]{3,2,1,0:T(8,128)} %bitcast.42, pred[3,16]{1,0:T(4,128)(4,1)S(1)} %get-tuple-element.7), kind=kLoop, calls=%fused_computation.6 | loop fusion | flops 6291456 | bytes 50331696 | tf_op jit(solution)/shard_map/jit(_take)/select_n | solution.py:80
  101.7 0.0 copy-done.2
  101.7 2.9 %convolution_bitcast_fusion = f32[1,16,512,256]{2,3,1,0:T(8,128)S(1)} fusion(bf16[16,256,256]{2,1,0:T(8,128)(2,1)} %bitcast.45, bf16[512,512]{1,0:T(8,128)(2,1)S(1)} %copy-done.2), kind=kOutput, calls=%fused_computation.10 | convolution fusion | flops 1073741824 | bytes 10747904 | tf_op jit(solution)/shard_map/kn,anc->akc/dot_general | solution.py:70
  104.6 4.1 %slice_bitcast_fusion.1 = (f32[16,256,256]{1,2,0:T(8,128)}, f32[16,256,256]{1,2,0:T(8,128)}) fusion(f32[1,16,512,256]{2,3,1,0:T(8,128)S(1)} %convolution_bitcast_fusion), kind=kLoop, calls=%fused_computation.9 | loop fusion | bytes 16777216 | tf_op jit(solution)/shard_map/mul | solution.py:39
  108.8 5.4 %copy.17 = f32[16,256,256]{2,1,0:T(8,128)} copy(f32[16,256,256]{1,2,0:T(8,128)} %get-tuple-element.4) | data formatting | bytes 8388608 | tf_op jit(solution)/shard_map/mul | solution.py:39
  114.1 5.4 %copy.18 = f32[16,256,256]{2,1,0:T(8,128)} copy(f32[16,256,256]{1,2,0:T(8,128)} %get-tuple-element.5) | data formatting | bytes 8388608 | tf_op jit(solution)/shard_map/mul | solution.py:39
  119.5 11.9 %subtract_select_fusion = (f32[3,16,256,256]{3,2,1,0:T(8,128)S(1)}, f32[3,16,256,256]{3,2,1,0:T(8,128)S(1)}) fusion(f32[3,16,512,256]{3,2,1,0:T(8,128)} %broadcast_select_fusion, f32[16,256,256]{2,1,0:T(8,128)} %copy.18, f32[16,256,256]{2,1,0:T(8,128)} %copy.17, pred[256]{0:T(512)(128)(4,1)S(1)} %iota_compare_fusion.2), kind=kLoop, calls=%fused_computation.3 | loop fusion | flops 25165824 | bytes 58720512 | tf_op jit(solution)/shard_map/jit(_where)/select_n | solution.py:39
  131.4 0.0 copy-start
  131.4 0.0 copy-start.4
  131.4 0.0 copy-start.6
  131.4 2.6 %fusion = f32[3,512,256]{2,1,0:T(8,128)S(1)} fusion(f32[3,16,256,256]{3,2,1,0:T(8,128)S(1)} %get-tuple-element.3, f32[3,16,256,256]{3,2,1,0:T(8,128)S(1)} %get-tuple-element.2, pred[3,16]{1,0:T(4,128)(4,1)S(1)} %get-tuple-element.6), kind=kLoop, calls=%fused_computation.2 | loop fusion | flops 18481152 | bytes 26738736 | tf_op jit(solution)/shard_map/reduce_sum | solution.py:82
  134.1 3.0 %convolution_bitcast_fusion.1 = f32[3,256,256]{2,1,0:T(8,128)S(1)} fusion(f32[3,512,256]{2,1,0:T(8,128)S(1)} %fusion, s32[512]{0:T(512)S(1)} %get-tuple-element.8, s32[512]{0:T(512)S(1)} %get-tuple-element.9, s32[256]{0:T(256)S(1)} %get-tuple-element.16, s32[256]{0:T(256)S(1)} %get-tuple-element.17, pred[256]{0:T(512)(128)(4,1)S(1)} %compare_and_fusion, ...), kind=kOutput, calls=%fused_computation.16 | convolution fusion | flops 607518720 | bytes 2367232 | tf_op jit(solution)/shard_map/nk,akc->anc/dot_general | solution.py:83
  137.1 0.0 copy-done
  137.1 0.0 copy-done.4
  137.1 0.0 copy-done.6
  137.1 0.8 fusion.16
  137.9 0.0 all-gather.5.cloned.1.call-update
  138.0 0.7 slice_bitcast_fusion.2
  138.7 89.3 %all-gather.5.cloned.1.call-done = bf16[512,8192]{1,0:T(8,128)(2,1)} async-done(((bf16[512,256]{1,0:T(8,128)(2,1)}), bf16[512,8192]{1,0:T(8,128)(2,1)}) %all-gather.5.cloned.1.call-update) | async-done | bytes 8388624 | tf_op jit(solution)/shard_map/all_gather | solution.py:92
  228.0 7.6 %convolution_convert_fusion = bf16[512,256]{1,0:T(8,128)(2,1)} fusion(bf16[512,8192]{1,0:T(8,128)(2,1)} %all-gather.5.cloned.1.call-done, bf16[8192,256]{1,0:T(8,128)(2,1)} %param.13), kind=kOutput, calls=%fused_computation.17 | convolution fusion | flops 2147614720 | bytes 12845056 | tf_op jit(solution)/shard_map/dot_general | solution.py:91
  (10 shorter events, 0.1 us)
Async XLA Ops:
  7.2 10.6 %copy-start.3 = (bf16[512,256]{1,0:T(8,128)(2,1)S(1)}, bf16[512,256]{1,0:T(8,128)(2,1)}, u32[]{:S(2)}) copy-start(bf16[512,256]{1,0:T(8,128)(2,1)} %param.10) | copy-start | bytes 786436
  7.2 12.4 %copy-start.5 = (s32[16]{0:T(128)S(1)}, s32[16]{0:T(128)}, u32[]{:S(2)}) copy-start(s32[16]{0:T(128)} %param.14) | copy-start | bytes 196
  7.2 12.5 %copy-start.7 = (s32[8]{0:T(128)S(1)}, s32[8]{0:T(128)}, u32[]{:S(2)}) copy-start(s32[8]{0:T(128)} %param.15) | copy-start | bytes 100
  10.3 49.1 %all-to-all-start = ((bf16[8,768,256]{2,1,0:T(8,128)(2,1)}), bf16[8,768,256]{2,1,0:T(8,128)(2,1)S(1)}, u32[]{:S(2)}, u32[]{:S(2)}) async-start(bf16[8,768,256]{2,1,0:T(8,128)(2,1)} %stack.2), calls=%async_computation | async-start | bytes 6291456 | tf_op jit(solution)/shard_map/all_to_all | solution.py:57
  17.7 84.0 %all-gather.3.cloned.1.call-start = ((), (), s32[]{:S(2)}) async-start(), calls=%async_computation.1 | async-start | bytes 2359296 | tf_op jit(solution)/shard_map/all_gather | solution.py:69
  19.5 208.5 %all-gather.5.cloned.1.call-start = ((), (), s32[]{:S(2)}) async-start(), calls=%async_computation.2 | async-start | bytes 8650752 | tf_op jit(solution)/shard_map/all_gather | solution.py:92
  59.6 2.8 %copy-start.1 = (bf16[512,512]{1,0:T(8,128)(2,1)S(1)}, bf16[512,512]{1,0:T(8,128)(2,1)}, u32[]{:S(2)}) copy-start(bf16[512,512]{1,0:T(8,128)(2,1)} %select_convert_fusion) | copy-start | bytes 1572868
  84.2 17.5 %copy-start.2 = (bf16[512,512]{1,0:T(8,128)(2,1)S(1)}, bf16[512,512]{1,0:T(8,128)(2,1)}, u32[]{:S(2)}) copy-start(bf16[512,512]{1,0:T(8,128)(2,1)} %select_convert_fusion) | copy-start | bytes 1572868
  131.4 5.7 %copy-start = (bf16[512,256]{1,0:T(8,128)(2,1)S(1)}, bf16[512,256]{1,0:T(8,128)(2,1)}, u32[]{:S(2)}) copy-start(bf16[512,256]{1,0:T(8,128)(2,1)} %multiply_convert_fusion) | copy-start | bytes 786436
  131.4 5.7 %copy-start.4 = (bf16[512,256]{1,0:T(8,128)(2,1)S(1)}, bf16[512,256]{1,0:T(8,128)(2,1)}, u32[]{:S(2)}) copy-start(bf16[512,256]{1,0:T(8,128)(2,1)} %param.8) | copy-start | bytes 786436
  131.4 5.7 %copy-start.6 = (f32[256]{0:T(256)S(1)}, f32[256]{0:T(256)}, u32[]{:S(2)}) copy-start(f32[256]{0:T(256)} %param.12) | copy-start | bytes 3076
Sparse Core Ops, SparseCore 0:
  21.8 73.8 all-gather.2
  138.1 89.8 all-gather.4
